TPU v7x, 256 devices: a whole 4x4x8 slice. The times are simulated.
256 devices in a mesh: fsdp: 16 (over x, y), seq: 16 (over z, core).
Axes of the slice: x: 4, y: 4, z: 8, core: 2. Of those that a mesh axis runs over, the one named last changes fastest.
Arguments:
- tokens: bfloat16 [65536, 2048], P(('fsdp', 'seq')), may hold values from -6 to 6
- seq_lengths: int32 [16, 4], P('fsdp'), may hold values from 1 to 2048, 4096 in all within a row
- in_weight: bfloat16 [2048, 6144], P(None, 'fsdp'), may hold values from -0.125 to 0.125
- short_filter: float32 [7, 6144], replicated, may hold values from -2.5 to 2.5
- long_filter: bfloat16 [128, 128], replicated, may hold values from -0.5 to 0.5
- out_weight: bfloat16 [2048, 2048], replicated, may hold values from -0.125 to 0.125
Outputs:
- mixed: bfloat16 [65536, 2048], P(('fsdp', 'seq'))
Inputs may be any that keep to these rules, and one draw needn't show every extreme that they name: `seq_lengths`: in each pack the 4 lengths sum to 4096 and the longest is exactly 2048.
All inputs are finite; a program needn't handle non-finite values.
Results may differ from a plain program's by a relative error of at most 0.0073.
Values may be sent and summed in bfloat16 or wider, within the bound.
No kernel may reach another device: no remote copies, remote signals or barrier semaphores. Data moves between devices by JAX's collectives and lax.ppermute only.
A program may use at most 128 MiB of HBM per device.

v0:
```python
import jax
import jax.numpy as jnp
from jax import lax
from jax.sharding import PartitionSpec as P


def from_behind(block, axis, distance):
    devices = range(lax.axis_size(axis))
    route = [(i - distance, i) for i in devices if i - distance in devices]
    return lax.ppermute(block, axis, route)


def positions(row_ids, seq_starts):
    seq_begin = jnp.max(
        jnp.where(seq_starts[None, :] <= row_ids[:, None], seq_starts[None, :], 0), axis=1
    )
    return row_ids - seq_begin


def featurize(extended, position, taps):
    width = taps.shape[0]
    rows = position.shape[0]
    total = jnp.zeros((rows, extended.shape[1]), jnp.float32)
    for tap_index in range(width):
        part = extended[width - 1 - tap_index : width - 1 - tap_index + rows].astype(jnp.float32)
        total = total + taps[tap_index] * jnp.where((position >= tap_index)[:, None], part, 0.0)
    return total


def tap_table(tap_ids, long_filter):
    filter_len = long_filter.shape[0]
    one_hot = (
        tap_ids[:, :, None] == jnp.arange(filter_len, dtype=jnp.int32)[None, None, :]
    ).astype(jnp.bfloat16)
    return jnp.einsum(
        "ijt,tg->ijg", one_hot, long_filter, preferred_element_type=jnp.float32
    ).astype(jnp.bfloat16)


def local(tokens, seq_lengths, in_weight, short_filter, long_filter, out_weight):
    row_count, channels = tokens.shape
    width = short_filter.shape[0]
    filter_len, group_count = long_filter.shape
    projected = jnp.dot(
        tokens,
        lax.all_gather(in_weight, "fsdp", axis=1, tiled=True),
        preferred_element_type=jnp.float32,
    ).astype(jnp.bfloat16)
    lengths_row = seq_lengths[0]
    seq_starts = jnp.cumsum(lengths_row) - lengths_row
    first_global = lax.axis_index("seq") * row_count
    row_ids = first_global + jnp.arange(row_count, dtype=jnp.int32)
    position = positions(row_ids, seq_starts)
    prev_tail = from_behind(projected[row_count - (width - 1) :], "seq", 1)
    extended = jnp.concatenate([prev_tail, projected], axis=0)
    featured = featurize(extended, position, short_filter)
    queries = featured[:, :channels]
    mixed_in = (featured[:, channels : 2 * channels] * featured[:, 2 * channels :]).astype(
        jnp.bfloat16
    )
    conv_tail = from_behind(mixed_in[row_count - (filter_len - 1) :], "seq", 1)
    window_all = jnp.concatenate([conv_tail, mixed_in], axis=0)
    out_rows = jnp.arange(filter_len, dtype=jnp.int32)[:, None]
    cur_tap = out_rows - jnp.arange(filter_len, dtype=jnp.int32)[None, :]
    prev_tap = out_rows + (filter_len - 1) - jnp.arange(filter_len - 1, dtype=jnp.int32)[None, :]
    cur_table = tap_table(cur_tap, long_filter)
    prev_table = tap_table(prev_tap, long_filter)
    per_group = channels // group_count
    pieces = []
    for block_id in range(row_count // filter_len):
        first_row = block_id * filter_len
        block_pos = position[first_row : first_row + filter_len]
        cur_kernel = jnp.where((cur_tap <= block_pos[:, None])[:, :, None], cur_table, 0.0)
        prev_kernel = jnp.where((prev_tap <= block_pos[:, None])[:, :, None], prev_table, 0.0)
        prev_src = window_all[first_row : first_row + filter_len - 1].reshape(
            filter_len - 1, group_count, per_group
        )
        cur_src = window_all[first_row + filter_len - 1 : first_row + 2 * filter_len - 1].reshape(
            filter_len, group_count, per_group
        )
        block_out = jnp.einsum(
            "ijg,jgc->igc", cur_kernel, cur_src, preferred_element_type=jnp.float32
        )
        block_out = block_out + jnp.einsum(
            "ijg,jgc->igc", prev_kernel, prev_src, preferred_element_type=jnp.float32
        )
        pieces.append(block_out.reshape(filter_len, channels))
    filtered = jnp.concatenate(pieces, axis=0)
    gated_out = (queries * filtered).astype(jnp.bfloat16)
    result = tokens.astype(jnp.float32) + jnp.dot(
        gated_out, out_weight, preferred_element_type=jnp.float32
    )
    return result.astype(jnp.bfloat16)


def solution(mesh):
    in_specs = (P(("fsdp", "seq"), None), P("fsdp", None), P(None, "fsdp"), P(), P(), P())
    out_specs = P(("fsdp", "seq"), None)
    return jax.shard_map(local, mesh=mesh, in_specs=in_specs, out_specs=out_specs, check_vma=False)
```

profile of v0, /device:TPU:1, one launch (start us, length us, event | category | flops | bytes accessed | tf_op | source)
XLA Modules:
  0.0 275.3 jit_solution(17743482276146317237)
XLA Ops:
  6.5 0.7 all-gather.2.cloned.1.call-update
  7.3 0.8 reduce-window_clone.1
  8.1 0.7 subtract_bitcast_fusion
  9.1 8.8 %broadcast_select_fusion.3 = (bf16[128,127,128]{2,0,1:T(8,128)(2,1)}, bf16[128,127,128]{2,0,1:T(8,128)(2,1)}) fusion(pred[128,127]{0,1:T(8,128)(4,1)S(1)} %get-tuple-element.30, pred[128,127]{0,1:T(8,128)(4,1)S(1)} %get-tuple-element.31, bf16[128,128]{1,0:T(8,128)(2,1)S(1)} %copy-done, s32[128,127]{0,1:T(8,128)S(1)} %iota_subtract_fusion), kind=kOutput, calls=%fused_computation.16 | convolution fusion | flops 540999680 | bytes 8453376 | tf_op jit(solution)/shard_map/ijt,tg->ijg/dot_general | solution.py:35
  17.9 10.4 %broadcast_select_fusion.1 = (bf16[128,128,128]{2,1,0:T(8,128)(2,1)}, bf16[128,128,128]{2,1,0:T(8,128)(2,1)}) fusion(pred[128,128]{1,0:T(8,128)(4,1)S(1)} %get-tuple-element.33, pred[128,128]{1,0:T(8,128)(4,1)S(1)} %get-tuple-element.32, bf16[128,128]{1,0:T(8,128)(2,1)S(1)} %copy-done, s32[128,128]{1,0:T(8,128)S(1)} %iota_subtract_fusion.1), kind=kOutput, calls=%fused_computation.13 | convolution fusion | flops 545259520 | bytes 8519680 | tf_op jit(solution)/shard_map/ijt,tg->ijg/dot_general | solution.py:35
  28.4 153.1 %all-gather.2.cloned.1.call-done = bf16[2048,6144]{1,0:T(8,128)(2,1)} async-done(((bf16[2048,384]{1,0:T(8,128)(2,1)}), bf16[2048,6144]{1,0:T(8,128)(2,1)}) %all-gather.2.cloned.1.call-update) | async-done | bytes 25165840 | tf_op jit(solution)/shard_map/all_gather | solution.py:46
  181.5 11.9 %convolution_convert_fusion = bf16[256,6144]{1,0:T(8,128)(2,1)S(1)} fusion(bf16[256,2048]{1,0:T(8,128)(2,1)} %param.6, bf16[2048,6144]{1,0:T(8,128)(2,1)} %all-gather.2.cloned.1.call-done), kind=kOutput, calls=%fused_computation.9 | convolution fusion | flops 6444023808 | bytes 29360128 | tf_op jit(solution)/shard_map/dot_general | solution.py:44
  193.4 4.6 %collective-permute-start = (bf16[6,6144]{1,0:T(8,128)(2,1)S(1)}, bf16[6,6144]{1,0:T(8,128)(2,1)S(1)}, u32[]{:S(2)}, u32[]{:S(2)}) collective-permute-start(bf16[6,6144]{1,0:T(8,128)(2,1)S(1)} %slice.92), channel_id=1, source_target_pairs={{0,1},{1,2},{2,3},{3,4},{4,5},{5,6},{6,7},{7,8},{8,9},{9,10},{10,1... | collective-permute-start | bytes 221192 | tf_op jit(solution)/shard_map/ppermute | solution.py:10
  198.1 6.7 %copy.32 = bf16[128,128,128]{1,0,2:T(8,128)(2,1)} copy(bf16[128,128,128]{2,1,0:T(8,128)(2,1)} %get-tuple-element.8) | data formatting | bytes 8388608 | tf_op jit(solution)/shard_map/jit(_where)/select_n | solution.py:73
  204.7 7.2 %copy.34 = bf16[128,127,128]{1,0,2:T(8,128)(2,1)} copy(bf16[128,127,128]{2,0,1:T(8,128)(2,1)} %get-tuple-element.10) | data formatting | bytes 8323072 | tf_op jit(solution)/shard_map/jit(_where)/select_n | solution.py:74
  211.9 6.7 %copy.28 = bf16[128,128,128]{1,0,2:T(8,128)(2,1)} copy(bf16[128,128,128]{2,1,0:T(8,128)(2,1)} %get-tuple-element.7) | data formatting | bytes 8388608 | tf_op jit(solution)/shard_map/jit(_where)/select_n | solution.py:73
  218.6 7.2 %copy.30 = bf16[128,127,128]{1,0,2:T(8,128)(2,1)} copy(bf16[128,127,128]{2,0,1:T(8,128)(2,1)} %get-tuple-element.9) | data formatting | bytes 8323072 | tf_op jit(solution)/shard_map/jit(_where)/select_n | solution.py:74
  225.8 9.8 %multiply_add_fusion = f32[256,6144]{1,0:T(8,128)S(1)} fusion(bf16[256,6144]{1,0:T(8,128)(2,1)S(1)} %convolution_convert_fusion, bf16[6,6144]{1,0:T(8,128)(2,1)S(1)} %collective-permute-done, f32[6144]{0:T(1024)S(1)} %bitcast.52, f32[6144]{0:T(1024)S(1)} %bitcast.53, f32[6144]{0:T(1024)S(1)} %bitcast.48, f32[6144]{0:T(1024)S(1)} %bitcast.49, ...), kind=kLoop, calls=%fused_computation.10 | loop fusion | flops 70778880 | bytes 9684736 | tf_op jit(solution)/shard_map/add | solution.py:26
  235.7 2.6 copy-done.2
  238.6 1.1 fusion.24
  240.3 2.4 collective-permute-start.1
  242.6 4.5 %fusion.29 = f32[128,16,128]{2,1,0:T(8,128)S(1)} fusion(bf16[128,128,16]{0,2,1:T(8,128)(2,1)S(1)} %bitcast.44, bf16[128,128,128]{1,0,2:T(8,128)(2,1)} %copy.32), kind=kOutput, calls=%fused_computation.62 | convolution fusion | flops 67108864 | bytes 5767168 | tf_op jit(solution)/shard_map/ijg,jgc->igc/dot_general | solution.py:81
  247.1 2.3 convolution_add_fusion.1
  249.4 1.4 copy.36
  251.0 4.5 %fusion.28 = f32[128,16,128]{2,1,0:T(8,128)S(1)} fusion(bf16[128,128,16]{0,2,1:T(8,128)(2,1)S(1)} %bitcast.46, bf16[128,128,128]{1,0,2:T(8,128)(2,1)} %copy.28), kind=kOutput, calls=%fused_computation.61 | convolution fusion | flops 67108864 | bytes 5767168 | tf_op jit(solution)/shard_map/ijg,jgc->igc/dot_general | solution.py:81
  255.5 0.3 copy.29
  255.8 4.4 %convolution_add_fusion.2 = f32[128,16,128]{2,1,0:T(8,128)S(1)} fusion(f32[128,16,128]{2,1,0:T(8,128)S(1)} %fusion.28, bf16[127,128,16]{0,2,1:T(8,128)(2,1)S(1)} %bitcast.45, bf16[128,127,128]{1,0,2:T(8,128)(2,1)} %copy.30), kind=kOutput, calls=%fused_computation.35 | convolution fusion | flops 66846720 | bytes 6778880 | tf_op jit(solution)/shard_map/ijg,jgc->igc/dot_general | solution.py:84
  260.2 0.4 copy.35
  260.6 7.9 %fusion.11 = bf16[256,2048]{1,0:T(8,128)(2,1)} fusion(bf16[2048,2048]{1,0:T(8,128)(2,1)} %param.11, bf16[256,2048]{1,0:T(8,128)(2,1)} %param.6, f32[256,6144]{1,0:T(8,128)} %copy-done.2, f32[128,2048]{1,0:T(8,128)} %copy.36, f32[128,2048]{1,0:T(8,128)S(1)} %copy.35), kind=kOutput, calls=%fused_computation.29 | convolution fusion | flops 2150629376 | bytes 14680064 | tf_op jit(solution)/shard_map/dot_general | solution.py:90
  (29 shorter events, 1.6 us)
Async XLA Ops:
  6.5 2.5 copy-start
  6.5 175.0 %all-gather.2.cloned.1.call-start = ((), (), s32[]{:S(2)}) async-start(), calls=%async_computation | async-start | bytes 26738688 | tf_op jit(solution)/shard_map/all_gather | solution.py:46
  17.9 10.4 %copy-start.4 = (f32[7,6144]{1,0:T(8,128)S(1)}, f32[7,6144]{1,0:T(8,128)}, u32[]{:S(2)}) copy-start(f32[7,6144]{1,0:T(8,128)} %param.9) | copy-start | bytes 516100
  193.4 32.4 %collective-permute-start = (bf16[6,6144]{1,0:T(8,128)(2,1)S(1)}, bf16[6,6144]{1,0:T(8,128)(2,1)S(1)}, u32[]{:S(2)}, u32[]{:S(2)}) collective-permute-start(bf16[6,6144]{1,0:T(8,128)(2,1)S(1)} %slice.92), channel_id=1, source_target_pairs={{0,1},{1,2},{2,3},{3,4},{4,5},{5,6},{6,7},{7,8},{8,9},{9,10},{10,1... | collective-permute-start | bytes 221192 | tf_op jit(solution)/shard_map/ppermute | solution.py:10
  235.7 2.6 copy-start.2
  240.3 6.8 %copy-start.3 = (bf16[128,127,128]{1,0,2:T(8,128)(2,1)S(1)}, bf16[128,127,128]{1,0,2:T(8,128)(2,1)}, u32[]{:S(2)}) copy-start(bf16[128,127,128]{1,0,2:T(8,128)(2,1)} %copy.34) | copy-start | bytes 12484612
  240.3 15.2 %collective-permute-start.1 = (bf16[127,2048]{1,0:T(8,128)(2,1)}, bf16[127,2048]{1,0:T(8,128)(2,1)S(1)}, u32[]{:S(2)}, u32[]{:S(2)}) collective-permute-start(bf16[127,2048]{1,0:T(8,128)(2,1)} %get-tuple-element.11), channel_id=1, source_target_pairs={{0,1},{1,2},{2,3},{3,4},{4,5},{5,6},{6,7},{7,8},{8,9},{9,10},{10,1... | collective-permute-start | bytes 1560584 | tf_op jit(solution)/shard_map/ppermute | solution.py:10
  260.6 7.9 %copy-start.1 = (bf16[128,128]{1,0:T(8,128)(2,1)S(1)}, bf16[128,128]{1,0:T(8,128)(2,1)}, u32[]{:S(2)}) copy-start(bf16[128,128]{1,0:T(8,128)(2,1)} %param.10) | copy-start | bytes 98308
Sparse Core Ops, SparseCore 0:
  9.8 171.6 all-gather.1
where the time goes:
time: 276 us; the launch traced here: 275 us
  waiting for transfers between devices  154 us (56%)
  matrix products  54.6 us (20%)
  local copies, waits for them, and re-layouts  34.5 us (12%)
  between operations  13.6 us (5%)
  other arithmetic  11.8 us (4%)
  starting transfers between devices  6.97 us (3%)
    all_gather x1, waiting for transfers between devices, local(): lax.all_gather(in_weight, 'fsdp', axis=1, tiled=True)  153 us
    dot_general x2, matrix products, tap_table(): jnp.einsum('ijt,tg->ijg', one_hot, long_filter, preferred_element_type=jn...  19.2 us
    select_n x2, local copies, waits for them, and re-layouts, local(): jnp.where((prev_tap <= block_pos[:, None])[:, :, None], prev_table, 0.0)  14.4 us
    select_n x2, local copies, waits for them, and re-layouts, local(): jnp.where((cur_tap <= block_pos[:, None])[:, :, None], cur_table, 0.0)  13.4 us
    dot_general x1, matrix products, local(): jnp.dot(tokens, lax.all_gather(in_weight, 'fsdp', axis=1, tiled=True), pr...  11.9 us
    add x1, other arithmetic, featurize(): total + taps[tap_index] * jnp.where((position >= tap_index)[:, None], par...  9.84 us
    dot_general x2, matrix products, local(): jnp.einsum('ijg,jgc->igc', cur_kernel, cur_src, preferred_element_type=jn...  8.91 us
    dot_general x1, matrix products, local(): jnp.dot(gated_out, out_weight, preferred_element_type=jnp.float32)  7.87 us
  transfers between devices with their start and end apart: 3, of which 1 were waited for; matrix products, arithmetic and copies ran while one was open for 22% of the time, Pallas kernels for 0%

commit v1 on v0

--- a/solution.py
+++ b/solution.py
@@ -43,7 +43,9 @@
     filter_len, group_count = long_filter.shape
     projected = jnp.dot(
         tokens,
-        lax.all_gather(in_weight, "fsdp", axis=1, tiled=True),
+        jnp.concatenate(
+            lax.all_to_all(jnp.stack([in_weight] * lax.axis_size("fsdp")), "fsdp", 0, 0), axis=1
+        ),
         preferred_element_type=jnp.float32,
     ).astype(jnp.bfloat16)
     lengths_row = seq_lengths[0]

time: 276 us -> 567 us (2.05)
  waiting for transfers between devices: 154 us -> 436 us
  between operations: 13.6 us -> 0.21 us
  local copies, waits for them, and re-layouts: 34.5 us -> 44.9 us
  starting transfers between devices: 6.97 us -> 15.7 us
    all_to_all x0 -> x1, waiting for transfers between devices: none -> 436 us  [local(): lax.all_to_all(jnp.stack([in_weight] * lax.axis_size('fsdp')), 'fsdp', 0, 0)]
    all_gather x1 -> x0, waiting for transfers between devices: 153 us -> none  [local(): lax.all_gather(in_weight, 'fsdp', axis=1, tiled=True)]
    another operation x0 -> x1, local copies, waits for them, and re-layouts: none -> 8.64 us  [local(): jnp.stack([in_weight] * lax.axis_size('fsdp'))]
    all_to_all x0 -> x1, starting transfers between devices: none -> 7.76 us  [local(): lax.all_to_all(jnp.stack([in_weight] * lax.axis_size('fsdp')), 'fsdp', 0, 0)]
  transfers between devices with their start and end apart: 3 -> 3, of which waited for: 1 -> 1; matrix products, arithmetic and copies ran while one was open for 22% -> 11% of each run, Pallas kernels for 0% -> 0%
where the time goes in v1:
time: 567 us; the launch traced here: 562 us
  waiting for transfers between devices  436 us (77%)
  matrix products  54.7 us (10%)
  local copies, waits for them, and re-layouts  44.9 us (8%)
  starting transfers between devices  15.7 us (3%)
  other arithmetic  10.5 us (2%)
    all_to_all x1, waiting for transfers between devices, local(): lax.all_to_all(jnp.stack([in_weight] * lax.axis_size('fsdp')), 'fsdp', 0, 0)  436 us
    dot_general x2, matrix products, tap_table(): jnp.einsum('ijt,tg->ijg', one_hot, long_filter, preferred_element_type=jn...  19.3 us
    select_n x2, local copies, waits for them, and re-layouts, local(): jnp.where((prev_tap <= block_pos[:, None])[:, :, None], prev_table, 0.0)  14.4 us
    select_n x2, local copies, waits for them, and re-layouts, local(): jnp.where((cur_tap <= block_pos[:, None])[:, :, None], cur_table, 0.0)  13.4 us
    dot_general x1, matrix products, local(): jnp.dot(tokens, jnp.concatenate(lax.all_to_all(jnp.stack([in_weight] * la...  11.9 us
  transfers between devices with their start and end apart: 3, of which 1 were waited for; matrix products, arithmetic and copies ran while one was open for 11% of the time, Pallas kernels for 0%

profile of v1, /device:TPU:1, one launch (start us, length us, event | category | flops | bytes accessed | tf_op | source)
XLA Modules:
  0.0 562.3 jit_solution(13287580985086296765)
XLA Ops:
  0.0 1.7 copy.28
  1.7 8.6 %stack.2 = bf16[16,2048,384]{1,2,0:T(8,128)(2,1)} broadcast(bf16[2048,384]{0,1:T(8,128)(2,1)S(1)} %copy.28), dimensions={1,2} | broadcast | bytes 26738688 | tf_op jit(solution)/shard_map/stack | solution.py:47
  10.4 7.8 %all-to-all-start = ((bf16[16,2048,384]{1,2,0:T(8,128)(2,1)}), bf16[16,2048,384]{1,2,0:T(8,128)(2,1)}, u32[]{:S(2)}, u32[]{:S(2)}) async-start(bf16[16,2048,384]{1,2,0:T(8,128)(2,1)} %stack.2), calls=%async_computation | async-start | bytes 50331648 | tf_op jit(solution)/shard_map/all_to_all | solution.py:47
  18.6 8.9 %broadcast_select_fusion.3 = (bf16[128,127,128]{2,0,1:T(8,128)(2,1)}, bf16[128,127,128]{2,0,1:T(8,128)(2,1)}) fusion(pred[128,127]{0,1:T(8,128)(4,1)S(1)} %get-tuple-element.30, pred[128,127]{0,1:T(8,128)(4,1)S(1)} %get-tuple-element.31, bf16[128,128]{1,0:T(8,128)(2,1)S(1)} %copy-done, s32[128,127]{0,1:T(8,128)S(1)} %iota_subtract_fusion), kind=kOutput, calls=%fused_computation.16 | convolution fusion | flops 540999680 | bytes 8453376 | tf_op jit(solution)/shard_map/ijt,tg->ijg/dot_general | solution.py:35
  27.5 10.4 %broadcast_select_fusion.1 = (bf16[128,128,128]{2,1,0:T(8,128)(2,1)}, bf16[128,128,128]{2,1,0:T(8,128)(2,1)}) fusion(pred[128,128]{1,0:T(8,128)(4,1)S(1)} %get-tuple-element.33, pred[128,128]{1,0:T(8,128)(4,1)S(1)} %get-tuple-element.32, bf16[128,128]{1,0:T(8,128)(2,1)S(1)} %copy-done, s32[128,128]{1,0:T(8,128)S(1)} %iota_subtract_fusion.1), kind=kOutput, calls=%fused_computation.13 | convolution fusion | flops 545259520 | bytes 8519680 | tf_op jit(solution)/shard_map/ijt,tg->ijg/dot_general | solution.py:35
  38.0 436.2 %all-to-all-done = bf16[16,2048,384]{1,2,0:T(8,128)(2,1)} async-done(((bf16[16,2048,384]{1,2,0:T(8,128)(2,1)}), bf16[16,2048,384]{1,2,0:T(8,128)(2,1)}, u32[]{:S(2)}, u32[]{:S(2)}) %all-to-all-start) | async-done | bytes 25165856 | tf_op jit(solution)/shard_map/all_to_all | solution.py:47
  474.2 11.9 %convolution_convert_fusion = bf16[256,6144]{1,0:T(8,128)(2,1)S(1)} fusion(bf16[256,2048]{1,0:T(8,128)(2,1)} %param.6, bf16[2048,6144]{0,1:T(8,128)(2,1)} %bitcast.3), kind=kOutput, calls=%fused_computation.9 | convolution fusion | flops 6444023808 | bytes 29360128 | tf_op jit(solution)/shard_map/dot_general | solution.py:44
  486.2 5.6 collective-permute-start
  491.8 6.7 %copy.34 = bf16[128,128,128]{1,0,2:T(8,128)(2,1)} copy(bf16[128,128,128]{2,1,0:T(8,128)(2,1)} %get-tuple-element.8) | data formatting | bytes 8388608 | tf_op jit(solution)/shard_map/jit(_where)/select_n | solution.py:75
  498.5 7.2 %copy.36 = bf16[128,127,128]{1,0,2:T(8,128)(2,1)} copy(bf16[128,127,128]{2,0,1:T(8,128)(2,1)} %get-tuple-element.10) | data formatting | bytes 8323072 | tf_op jit(solution)/shard_map/jit(_where)/select_n | solution.py:76
  505.7 6.7 %copy.30 = bf16[128,128,128]{1,0,2:T(8,128)(2,1)} copy(bf16[128,128,128]{2,1,0:T(8,128)(2,1)} %get-tuple-element.7) | data formatting | bytes 8388608 | tf_op jit(solution)/shard_map/jit(_where)/select_n | solution.py:75
  512.4 7.2 %copy.32 = bf16[128,127,128]{1,0,2:T(8,128)(2,1)} copy(bf16[128,127,128]{2,0,1:T(8,128)(2,1)} %get-tuple-element.9) | data formatting | bytes 8323072 | tf_op jit(solution)/shard_map/jit(_where)/select_n | solution.py:76
  519.6 9.8 %multiply_add_fusion = f32[256,6144]{1,0:T(8,128)S(1)} fusion(bf16[256,6144]{1,0:T(8,128)(2,1)S(1)} %convolution_convert_fusion, bf16[6,6144]{1,0:T(8,128)(2,1)S(1)} %collective-permute-done, f32[6144]{0:T(1024)S(1)} %bitcast.55, f32[6144]{0:T(1024)S(1)} %bitcast.56, f32[6144]{0:T(1024)S(1)} %bitcast.51, f32[6144]{0:T(1024)S(1)} %bitcast.52, ...), kind=kLoop, calls=%fused_computation.10 | loop fusion | flops 70778880 | bytes 9684736 | tf_op jit(solution)/shard_map/add | solution.py:26
  529.4 2.6 copy-done.2
  532.4 1.1 fusion.24
  534.0 2.4 collective-permute-start.1
  536.4 4.5 fusion.29
  540.9 2.3 convolution_add_fusion.1
  543.2 1.4 copy.38
  544.8 4.5 fusion.28
  549.3 0.3 copy.31
  549.6 4.4 convolution_add_fusion.2
  554.0 0.4 copy.37
  554.4 7.9 %fusion.11 = bf16[256,2048]{1,0:T(8,128)(2,1)} fusion(bf16[2048,2048]{1,0:T(8,128)(2,1)} %param.11, bf16[256,2048]{1,0:T(8,128)(2,1)} %param.6, f32[256,6144]{1,0:T(8,128)} %copy-done.2, f32[128,2048]{1,0:T(8,128)} %copy.38, f32[128,2048]{1,0:T(8,128)S(1)} %copy.37), kind=kOutput, calls=%fused_computation.29 | convolution fusion | flops 2150629376 | bytes 14680064 | tf_op jit(solution)/shard_map/dot_general | solution.py:92
  (32 shorter events, 1.8 us)
Async XLA Ops:
  0.0 18.6 %copy-start = (bf16[128,128]{1,0:T(8,128)(2,1)S(1)}, bf16[128,128]{1,0:T(8,128)(2,1)}, u32[]{:S(2)}) copy-start(bf16[128,128]{1,0:T(8,128)(2,1)} %param.10) | copy-start | bytes 98308
  10.4 7.8 %copy-start.5 = (s32[1,4]{1,0:T(1,128)S(1)}, s32[1,4]{1,0:T(1,128)}, u32[]{:S(2)}) copy-start(s32[1,4]{1,0:T(1,128)} %param.7) | copy-start | bytes 52
  10.4 463.9 %all-to-all-start = ((bf16[16,2048,384]{1,2,0:T(8,128)(2,1)}), bf16[16,2048,384]{1,2,0:T(8,128)(2,1)}, u32[]{:S(2)}, u32[]{:S(2)}) async-start(bf16[16,2048,384]{1,2,0:T(8,128)(2,1)} %stack.2), calls=%async_computation | async-start | bytes 50331648 | tf_op jit(solution)/shard_map/all_to_all | solution.py:47
  27.5 10.4 %copy-start.4 = (f32[7,6144]{1,0:T(8,128)S(1)}, f32[7,6144]{1,0:T(8,128)}, u32[]{:S(2)}) copy-start(f32[7,6144]{1,0:T(8,128)} %param.9) | copy-start | bytes 516100
  486.2 33.4 %collective-permute-start = (bf16[6,6144]{1,0:T(8,128)(2,1)S(1)}, bf16[6,6144]{1,0:T(8,128)(2,1)S(1)}, u32[]{:S(2)}, u32[]{:S(2)}) collective-permute-start(bf16[6,6144]{1,0:T(8,128)(2,1)S(1)} %slice.92), channel_id=1, source_target_pairs={{0,1},{1,2},{2,3},{3,4},{4,5},{5,6},{6,7},{7,8},{8,9},{9,10},{10,1... | collective-permute-start | bytes 221192 | tf_op jit(solution)/shard_map/ppermute | solution.py:10
  529.4 2.6 copy-start.2
  534.0 6.8 %copy-start.3 = (bf16[128,127,128]{1,0,2:T(8,128)(2,1)S(1)}, bf16[128,127,128]{1,0,2:T(8,128)(2,1)}, u32[]{:S(2)}) copy-start(bf16[128,127,128]{1,0,2:T(8,128)(2,1)} %copy.36) | copy-start | bytes 12484612
  534.0 15.2 %collective-permute-start.1 = (bf16[127,2048]{1,0:T(8,128)(2,1)}, bf16[127,2048]{1,0:T(8,128)(2,1)S(1)}, u32[]{:S(2)}, u32[]{:S(2)}) collective-permute-start(bf16[127,2048]{1,0:T(8,128)(2,1)} %get-tuple-element.11), channel_id=1, source_target_pairs={{0,1},{1,2},{2,3},{3,4},{4,5},{5,6},{6,7},{7,8},{8,9},{9,10},{10,1... | collective-permute-start | bytes 1560584 | tf_op jit(solution)/shard_map/ppermute | solution.py:10
  554.4 7.9 %copy-start.1 = (bf16[128,128]{1,0:T(8,128)(2,1)S(1)}, bf16[128,128]{1,0:T(8,128)(2,1)}, u32[]{:S(2)}) copy-start(bf16[128,128]{1,0:T(8,128)(2,1)} %param.10) | copy-start | bytes 98308
